TPU v7x, 128 devices: a whole 4x4x4 slice. The times are simulated.
128 devices in a mesh: section: 16 (over z_lo, x, core), ctx: 8 (over z_hi, y).
Axes of the slice: x: 4, y: 4, z: 4 (z_hi: 2, z_lo: 2; z = z_hi * 2 + z_lo), core: 2. Of those that a mesh axis runs over, the one named last changes fastest.
Arguments:
- sent_fwd: bfloat16 [16, 1024, 4096], P('section', 'ctx'), may hold values from -6 to 6
- sent_grad: bfloat16 [16, 1024, 4096], P('section', 'ctx'), may hold values from -6 to 6
- saved_bwd: bfloat16 [16, 1024, 4096], P('section', 'ctx'), may hold values from -6 to 6
- norm_gain: float32 [16, 4096], P('section'), may hold values from 0.5 to 1.5
- key_proj: bfloat16 [16, 4096, 512], P('section')
- value_proj: bfloat16 [16, 4096, 512], P('section'), may hold values from -0.09375 to 0.09375
- seg_fwd: int32 [1024], replicated, may hold values from 0 to 3, never falling along the last dimension, each value on 1 to 512 neighbouring positions
- seg_bwd: int32 [1024], replicated, may hold values from 0 to 3, never falling along the last dimension, each value on 1 to 512 neighbouring positions
Outputs:
- fwd_out: bfloat16 [16, 1024, 4096], P('section', 'ctx')
- grad_out: bfloat16 [16, 1024, 4096], P('section', 'ctx')
Inputs may be any that keep to these rules, and one draw needn't show every extreme that they name: `seg_fwd`: segment ids never fall along the sequence, each segment has 1 to 512 positions and one has exactly 512. `seg_bwd`: segment ids never fall along the sequence, each segment has 1 to 512 positions and one has exactly 512.
All inputs are finite; a program needn't handle non-finite values.
Results may differ from a plain program's by a relative error of at most 0.02.
The roundings to bfloat16 on the way count: a program that leaves them out, or rounds other values in their place, can miss the bound.
Values may be sent and summed in bfloat16 or wider, within the bound.
No kernel may reach another device: no remote copies, remote signals or barrier semaphores. Data moves between devices by JAX's collectives and lax.ppermute only.
A program may use at most 128 MiB of HBM per device.

v0:
```python
import jax
import jax.numpy as jnp
from jax import lax
from jax.sharding import PartitionSpec as P

HD = 128
EPSILON = 1e-05
NEGATIVE = -1e30


def shifted(block, axis, distance):
    devices = range(lax.axis_size(axis))
    route = [((i - distance) % len(devices), i) for i in devices]
    return lax.ppermute(block, axis, route)


def normalize(inputs, gain):
    wide = inputs.astype(jnp.float32)
    inverse = lax.rsqrt(jnp.mean(wide * wide, axis=-1, keepdims=True) + EPSILON)
    return (wide * inverse * gain, wide, inverse)


def body(sent_fwd, sent_grad, saved_bwd, norm_gain, key_proj, value_proj, seg_fwd, seg_bwd):
    tok_rows = sent_fwd.shape[1]
    width = sent_fwd.shape[2]
    kv_width = key_proj.shape[2]
    heads = width // HD
    kv_heads = kv_width // HD
    group_size = heads // kv_heads
    scale_factor = HD ** (-0.5)
    offset = lax.axis_index("ctx") * tok_rows
    query_pos = offset + jnp.arange(tok_rows, dtype=jnp.int32)
    gain = norm_gain[0]
    key_weight = key_proj[0]
    value_weight = value_proj[0]
    arrived = shifted(sent_fwd, "section", 1)[0]
    upstream = shifted(sent_grad, "section", -1)[0]

    def layer_parts(inputs):
        normed, wide, inverse = normalize(inputs, gain)
        flat = normed.astype(jnp.bfloat16)
        keys = jnp.dot(flat, key_weight, preferred_element_type=jnp.float32).astype(jnp.bfloat16)
        values = jnp.dot(flat, value_weight, preferred_element_type=jnp.float32).astype(
            jnp.bfloat16
        )
        return (flat.reshape(tok_rows, heads, HD), keys, values, wide, inverse)

    fwd_query, fwd_keys, fwd_values, fwd_wide, fwd_inverse = layer_parts(arrived)
    bwd_query, bwd_keys, bwd_values, bwd_wide, bwd_inverse = layer_parts(saved_bwd[0])
    seg_query_fwd = lax.dynamic_slice_in_dim(seg_fwd, offset, tok_rows)
    key_piece = lax.all_gather(fwd_keys, "ctx", axis=0, tiled=True)
    value_piece = lax.all_gather(fwd_values, "ctx", axis=0, tiled=True)
    count_rows = key_piece.shape[0]
    key_pos = jnp.arange(count_rows, dtype=jnp.int32)
    allowed = (key_pos[None, :] <= query_pos[:, None]) & (
        seg_query_fwd[:, None] == seg_fwd[None, :]
    )
    run_max = jnp.full((heads, tok_rows), NEGATIVE, jnp.float32)
    new_max = []
    new_total = []
    new_acc = []
    for forward_group_idx in range(kv_heads):
        forward_head_slice = slice(
            forward_group_idx * group_size, (forward_group_idx + 1) * group_size
        )
        forward_feat_slice = slice(forward_group_idx * HD, (forward_group_idx + 1) * HD)
        forward_scores = (
            jnp.einsum(
                "tgd,sd->gts",
                fwd_query[:, forward_head_slice],
                key_piece[:, forward_feat_slice],
                preferred_element_type=jnp.float32,
            )
            * scale_factor
        )
        forward_scores = jnp.where(allowed[None], forward_scores, NEGATIVE)
        old_max = run_max[forward_head_slice]
        top_max = jnp.maximum(old_max, jnp.max(forward_scores, axis=-1))
        forward_expo = jnp.where(allowed[None], jnp.exp(forward_scores - top_max[:, :, None]), 0.0)
        new_max.append(top_max)
        new_total.append(jnp.sum(forward_expo, axis=-1))
        product = jnp.einsum(
            "gts,sd->gtd",
            forward_expo.astype(jnp.bfloat16),
            value_piece[:, forward_feat_slice],
            preferred_element_type=jnp.float32,
        )
        new_acc.append(product)
    bwd_key_all, bwd_value_all = (
        lax.all_gather(bwd_keys, "ctx", axis=0, tiled=True),
        lax.all_gather(bwd_values, "ctx", axis=0, tiled=True),
    )
    attended = jnp.concatenate(new_acc, axis=0) / jnp.concatenate(new_total, axis=0)[:, :, None]
    attended = jnp.transpose(attended, (1, 0, 2)).reshape(tok_rows, width)
    fwd_out = (arrived.astype(jnp.float32) + attended).astype(jnp.bfloat16)
    seq_len = bwd_key_all.shape[0]
    key_pos = jnp.arange(seq_len, dtype=jnp.int32)
    seg_query_bwd = lax.dynamic_slice_in_dim(seg_bwd, offset, tok_rows)
    allowed = (key_pos[None, :] <= query_pos[:, None]) & (
        seg_query_bwd[:, None] == seg_bwd[None, :]
    )
    grad_heads = upstream.reshape(tok_rows, heads, HD)
    dquery_parts, dkey_parts, dvalue_parts = ([], [], [])
    for group_idx in range(kv_heads):
        head_slice = slice(group_idx * group_size, (group_idx + 1) * group_size)
        feat_slice = slice(group_idx * HD, (group_idx + 1) * HD)
        query_grp = bwd_query[:, head_slice]
        key_grp = bwd_key_all[:, feat_slice]
        value_grp = bwd_value_all[:, feat_slice]
        grad_grp = grad_heads[:, head_slice]
        scores = (
            jnp.einsum("tgd,sd->gts", query_grp, key_grp, preferred_element_type=jnp.float32)
            * scale_factor
        )
        scores = jnp.where(allowed[None], scores, NEGATIVE)
        rowmax = jnp.max(scores, axis=-1, keepdims=True)
        expo = jnp.where(allowed[None], jnp.exp(scores - rowmax), 0.0)
        total = jnp.sum(expo, axis=-1, keepdims=True)
        probs = expo / total
        dprob = jnp.einsum("tgd,sd->gts", grad_grp, value_grp, preferred_element_type=jnp.float32)
        delta = jnp.sum(probs * dprob, axis=-1, keepdims=True)
        dscore_b = (probs * (dprob - delta)).astype(jnp.bfloat16)
        dquery_parts.append(
            jnp.einsum("gts,sd->tgd", dscore_b, key_grp, preferred_element_type=jnp.float32)
            * scale_factor
        )
        probs_b = probs.astype(jnp.bfloat16)
        dkey_parts.append(
            jnp.einsum("gts,tgd->sd", dscore_b, query_grp, preferred_element_type=jnp.float32)
            * scale_factor
        )
        dvalue_parts.append(
            jnp.einsum("gts,tgd->sd", probs_b, grad_grp, preferred_element_type=jnp.float32)
        )
    dquery = jnp.concatenate(dquery_parts, axis=1).reshape(tok_rows, width)
    dkey_terms = jnp.concatenate(dkey_parts, axis=1)
    dvalue_terms = jnp.concatenate(dvalue_parts, axis=1)
    dkeys, dvalues = (
        lax.psum_scatter(
            dkey_terms.astype(jnp.bfloat16), "ctx", scatter_dimension=0, tiled=True
        ).astype(jnp.float32),
        lax.psum_scatter(
            dvalue_terms.astype(jnp.bfloat16), "ctx", scatter_dimension=0, tiled=True
        ).astype(jnp.float32),
    )
    dnormed = dquery + jnp.dot(
        dkeys.astype(jnp.bfloat16), jnp.transpose(key_weight), preferred_element_type=jnp.float32
    )
    dnormed = dnormed + jnp.dot(
        dvalues.astype(jnp.bfloat16),
        jnp.transpose(value_weight),
        preferred_element_type=jnp.float32,
    )
    scaled = gain * dnormed
    grad_in = bwd_inverse * scaled - bwd_wide * bwd_inverse**3 * jnp.mean(
        bwd_wide * scaled, axis=-1, keepdims=True
    )
    grad_out = (upstream.astype(jnp.float32) + grad_in).astype(jnp.bfloat16)
    return (fwd_out[None], grad_out[None])


def solution(mesh):
    placed = (
        P("section", "ctx", None),
        P("section", "ctx", None),
        P("section", "ctx", None),
        P("section", None),
        P("section", None, None),
        P("section", None, None),
        P(),
        P(),
    )
    return jax.shard_map(
        body,
        mesh=mesh,
        in_specs=placed,
        out_specs=(P("section", "ctx", None), P("section", "ctx", None)),
        check_vma=False,
    )
```

profile of v0, /device:TPU:0, one launch (start us, length us, event | category | flops | bytes accessed | tf_op | source)
XLA Modules:
  0.0 373.6 jit_solution(17284572037392446250)
XLA Ops:
  9.5 3.9 %fusion.121 = bf16[128,512]{1,0:T(8,128)(2,1)} fusion(bf16[1,4096,512]{2,1,0:T(8,128)(2,1)} %param.12, bf16[1,128,4096]{2,1,0:T(8,128)(2,1)} %param.10, f32[128]{0:T(128)S(1)} %get-tuple-element.12, f32[4096]{0:T(1024)} %bitcast.352), kind=kOutput, calls=%fused_computation.149 | convolution fusion | flops 539033600 | bytes 5390848 | tf_op jit(solution)/shard_map/dot_general | solution.py:42
  13.6 3.6 fusion.127
  17.3 12.7 %collective-permute-done = bf16[1,128,4096]{2,1,0:T(8,128)(2,1)S(1)} collective-permute-done((bf16[1,128,4096]{2,1,0:T(8,128)(2,1)S(1)}, bf16[1,128,4096]{2,1,0:T(8,128)(2,1)S(1)}, u32[]{:S(2)}, u32[]{:S(2)}) %collective-permute-start) | collective-permute-done | bytes 1048608 | tf_op jit(solution)/shard_map/ppermute | solution.py:14
  30.3 3.6 fusion.118
  43.7 3.6 fusion.124
  47.4 4.2 %multiply_convert_fusion = (bf16[128,32,128]{2,0,1:T(8,128)(2,1)}, bf16[128,32,128]{2,0,1:T(8,128)(2,1)}) fusion(f32[128,32,128]{2,0,1:T(8,128)} %copy.40, f32[128]{0:T(128)S(1)} %get-tuple-element.12, f32[32,128]{1,0:T(8,128)S(1)} %bitcast.356, f32[128,32,128]{2,0,1:T(8,128)} %copy.29, f32[128]{0:T(128)S(1)} %add_rsqrt_fusion.1), kind=kLoop, calls=%fused_computation.95 | loop fusion | flops 3145728 | bytes 6308864 | tf_op jit(solution)/shard_map/convert_element_type | solution.py:41
  53.4 10.2 %all-gather.9.cloned.1.call-done = bf16[1024,512]{1,0:T(8,128)(2,1)} async-done(((bf16[128,512]{1,0:T(8,128)(2,1)}), bf16[1024,512]{1,0:T(8,128)(2,1)}) %all-gather.9.cloned.1.call-update) | async-done | bytes 1048592 | tf_op jit(solution)/shard_map/all_gather | solution.py:90
  63.6 4.7 %fusion.224 = (f32[8,128]{1,0:T(8,128)S(1)}, f32[8,128,1024]{1,2,0:T(8,128)}) fusion(pred[128,1024]{0,1:T(8,128)(4,1)S(1)} %get-tuple-element.13, bf16[128,32,128]{2,0,1:T(8,128)(2,1)} %get-tuple-element.9, bf16[1024,512]{1,0:T(8,128)(2,1)} %all-gather.9.cloned.1.call-done), kind=kOutput, calls=%fused_computation.247 | convolution fusion | flops 273679360 | bytes 4984832 | tf_op jit(solution)/shard_map/sub | solution.py:117
  68.3 44.6 %all-gather.11.cloned.1.call-done = bf16[1024,512]{1,0:T(8,128)(2,1)} async-done(((bf16[128,512]{1,0:T(8,128)(2,1)}), bf16[1024,512]{1,0:T(8,128)(2,1)}) %all-gather.11.cloned.1.call-update) | async-done | bytes 1048592 | tf_op jit(solution)/shard_map/all_gather | solution.py:91
  112.9 3.2 fusion.8
  120.1 5.5 %fusion.219 = (f32[8,128]{1,0:T(8,128)}, f32[8,128,1024]{1,2,0:T(8,128)}) fusion(pred[128,1024]{0,1:T(8,128)(4,1)} %copy-done.26, bf16[128,32,128]{2,0,1:T(8,128)(2,1)} %get-tuple-element.9, bf16[1024,512]{1,0:T(8,128)(2,1)} %all-gather.9.cloned.1.call-done), kind=kOutput, calls=%fused_computation.246 | convolution fusion | flops 273679360 | bytes 4984832 | tf_op jit(solution)/shard_map/sub | solution.py:117
  125.5 3.2 fusion.5
  133.4 5.4 %fusion.229 = (f32[8,128]{1,0:T(8,128)}, f32[8,128,1024]{1,2,0:T(8,128)}) fusion(pred[128,1024]{0,1:T(8,128)(4,1)} %copy-done.26, bf16[128,32,128]{2,0,1:T(8,128)(2,1)} %get-tuple-element.9, bf16[1024,512]{1,0:T(8,128)(2,1)} %all-gather.9.cloned.1.call-done), kind=kOutput, calls=%fused_computation.248 | convolution fusion | flops 273679360 | bytes 4984832 | tf_op jit(solution)/shard_map/sub | solution.py:117
  138.8 3.2 fusion.11
  144.3 5.4 %fusion.234 = (f32[8,128]{1,0:T(8,128)}, f32[8,128,1024]{1,2,0:T(8,128)}) fusion(pred[128,1024]{0,1:T(8,128)(4,1)} %copy-done.26, bf16[128,32,128]{2,0,1:T(8,128)(2,1)} %get-tuple-element.9, bf16[1024,512]{1,0:T(8,128)(2,1)} %all-gather.9.cloned.1.call-done), kind=kOutput, calls=%fused_computation.249 | convolution fusion | flops 273679360 | bytes 4984832 | tf_op jit(solution)/shard_map/sub | solution.py:117
  149.8 3.4 fusion.14
  171.1 3.2 fusion.102
  187.9 3.2 fusion.37
  191.2 18.2 %all-gather.7.cloned.1.call-done = bf16[1024,512]{1,0:T(8,128)(2,1)} async-done(((bf16[128,512]{1,0:T(8,128)(2,1)}), bf16[1024,512]{1,0:T(8,128)(2,1)}) %all-gather.7.cloned.1.call-update) | async-done | bytes 1048592 | tf_op jit(solution)/shard_map/all_gather | solution.py:52
  209.4 3.5 fusion.72
  226.0 59.2 %reduce-scatter.3.cloned.1.call-done = bf16[128,512]{1,0:T(8,128)(2,1)} async-done(((bf16[1024,512]{1,0:T(8,128)(2,1)}), bf16[128,512]{1,0:T(8,128)(2,1)}) %reduce-scatter.3.cloned.1.call-update) | async-done | bytes 131088 | tf_op jit(solution)/shard_map/reduce_scatter | solution.py:139
  285.1 5.7 %convolution_add_fusion.1 = f32[128,4096]{1,0:T(8,128)} fusion(f32[128,4096]{1,0:T(8,128)} %copy.54, bf16[128,512]{1,0:T(8,128)(2,1)} %reduce-scatter.3.cloned.1.call-done, bf16[1,4096,512]{2,1,0:T(8,128)(2,1)} %param.12), kind=kOutput, calls=%fused_computation.6 | convolution fusion | flops 537395200 | bytes 8519680 | tf_op jit(solution)/shard_map/dot_general | solution.py:146
  290.9 69.5 %reduce-scatter.5.cloned.1.call-done = bf16[128,512]{1,0:T(8,128)(2,1)} async-done(((bf16[1024,512]{1,0:T(8,128)(2,1)}), bf16[128,512]{1,0:T(8,128)(2,1)}) %reduce-scatter.5.cloned.1.call-update) | async-done | bytes 131088 | tf_op jit(solution)/shard_map/reduce_scatter | solution.py:142
  360.4 4.5 %fusion.47 = (f32[128]{0:T(128)S(1)}, f32[128,4096]{1,0:T(8,128)S(1)}) fusion(bf16[1,128,4096]{2,1,0:T(8,128)(2,1)S(1)} %copy-done, f32[128,4096]{1,0:T(8,128)} %convolution_add_fusion.1, bf16[128,512]{1,0:T(8,128)(2,1)} %reduce-scatter.5.cloned.1.call-done, bf16[1,4096,512]{2,1,0:T(8,128)(2,1)} %param.13, f32[4096]{0:T(1024)S(1)} %bitcast.357), kind=kOutput, calls=%fused_computation.79 | convolution fusion | flops 539492224 | bytes 9585152 | tf_op jit(solution)/shard_map/dot_general | solution.py:149
  (146 shorter events, 71.2 us)
Async XLA Ops:
  7.2 6.4 %copy-start = (bf16[1,128,4096]{2,1,0:T(8,128)(2,1)S(1)}, bf16[1,128,4096]{2,1,0:T(8,128)(2,1)}, u32[]{:S(2)}) copy-start(bf16[1,128,4096]{2,1,0:T(8,128)(2,1)} %param.10) | copy-start | bytes 3145732
  7.2 6.4 %copy-start.27 = (f32[1,4096]{1,0:T(1,128)S(1)}, f32[1,4096]{1,0:T(1,128)}, u32[]{:S(2)}) copy-start(f32[1,4096]{1,0:T(1,128)} %param.11) | copy-start | bytes 49156
  7.2 6.3 %copy-start.39 = (bf16[1,128,4096]{2,1,0:T(8,128)(2,1)S(1)}, bf16[1,128,4096]{2,1,0:T(8,128)(2,1)}, u32[]{:S(2)}) copy-start(bf16[1,128,4096]{2,1,0:T(8,128)(2,1)} %param.8) | copy-start | bytes 3145732
  7.2 56.4 %all-gather.9.cloned.1.call-start = ((), (), s32[]{:S(2)}) async-start(), calls=%async_computation.4 | async-start | bytes 1179648 | tf_op jit(solution)/shard_map/all_gather | solution.py:90
  9.5 37.9 %copy-start.36 = (f32[128]{0:T(128)}, f32[128]{0:T(128)S(1)}, u32[]{:S(2)}) copy-start(f32[128]{0:T(128)S(1)} %get-tuple-element.12) | copy-start | bytes 1540
  13.4 99.4 %all-gather.11.cloned.1.call-start = ((), (), s32[]{:S(2)}) async-start(), calls=%async_computation.5 | async-start | bytes 1179648 | tf_op jit(solution)/shard_map/all_gather | solution.py:91
  13.5 16.5 %collective-permute-start = (bf16[1,128,4096]{2,1,0:T(8,128)(2,1)S(1)}, bf16[1,128,4096]{2,1,0:T(8,128)(2,1)S(1)}, u32[]{:S(2)}, u32[]{:S(2)}) collective-permute-start(bf16[1,128,4096]{2,1,0:T(8,128)(2,1)S(1)} %copy-done.39), channel_id=1, source_target_pairs={{120,0},{0,8},{8,16},{16,24},{24,32},{32,40},{40,48},{48,56},{56,6... | collective-permute-start | bytes 3145736 | tf_op jit(solution)/shard_map/ppermute | solution.py:14
  17.2 161.9 %all-gather.5.cloned.1.call-start = ((), (), s32[]{:S(2)}) async-start(), calls=%async_computation.2 | async-start | bytes 1179648 | tf_op jit(solution)/shard_map/all_gather | solution.py:51
  30.3 5.4 %copy-start.29 = (s32[1024]{0:T(1024)S(1)}, s32[1024]{0:T(1024)}, u32[]{:S(2)}) copy-start(s32[1024]{0:T(1024)} %param.14) | copy-start | bytes 12292
  30.3 5.5 %copy-start.28 = (s32[1024]{0:T(1024)S(1)}, s32[1024]{0:T(1024)}, u32[]{:S(2)}) copy-start(s32[1024]{0:T(1024)} %param.15) | copy-start | bytes 12292
  34.0 175.4 %all-gather.7.cloned.1.call-start = ((), (), s32[]{:S(2)}) async-start(), calls=%async_computation.3 | async-start | bytes 1179648 | tf_op jit(solution)/shard_map/all_gather | solution.py:52
  34.0 17.6 %collective-permute-start.1 = (bf16[1,128,4096]{2,1,0:T(8,128)(2,1)}, bf16[1,128,4096]{2,1,0:T(8,128)(2,1)S(1)}, u32[]{:S(2)}, u32[]{:S(2)}) collective-permute-start(bf16[1,128,4096]{2,1,0:T(8,128)(2,1)} %param.9), channel_id=1, source_target_pairs={{8,0},{16,8},{24,16},{32,24},{40,32},{48,40},{56,48},{64,56},{72,6... | collective-permute-start | bytes 3145736 | tf_op jit(solution)/shard_map/ppermute | solution.py:14
  39.2 24.4 %copy-start.26 = (pred[128,1024]{0,1:T(8,128)(4,1)}, pred[128,1024]{0,1:T(8,128)(4,1)S(1)}, u32[]{:S(2)}) copy-start(pred[128,1024]{0,1:T(8,128)(4,1)S(1)} %get-tuple-element.13) | copy-start | bytes 393220
  47.3 237.8 %reduce-scatter.3.cloned.1.call-start = ((), (), s32[]{:S(2)}) async-start(), calls=%async_computation.6 | async-start | bytes 1179648 | tf_op jit(solution)/shard_map/reduce_scatter | solution.py:139
  68.3 47.8 %copy-start.33 = (f32[8,128]{1,0:T(8,128)}, f32[8,128]{1,0:T(8,128)S(1)}, u32[]{:S(2)}) copy-start(f32[8,128]{1,0:T(8,128)S(1)} %get-tuple-element.22) | copy-start | bytes 12292
  149.8 4.6 %copy-start.15 = (f32[8,128,1024]{1,2,0:T(8,128)S(1)}, f32[8,128,1024]{1,2,0:T(8,128)}, u32[]{:S(2)}) copy-start(f32[8,128,1024]{1,2,0:T(8,128)} %get-tuple-element.31) | copy-start | bytes 12582916
  149.8 4.6 %copy-start.34 = (f32[8,128]{1,0:T(8,128)S(1)}, f32[8,128]{1,0:T(8,128)}, u32[]{:S(2)}) copy-start(f32[8,128]{1,0:T(8,128)} %get-tuple-element.30) | copy-start | bytes 12292
  161.1 199.3 %reduce-scatter.5.cloned.1.call-start = ((), (), s32[]{:S(2)}) async-start(), calls=%async_computation.7 | async-start | bytes 1179648 | tf_op jit(solution)/shard_map/reduce_scatter | solution.py:142
  161.1 4.5 %copy-start.8 = (bf16[8,128,1024]{1,2,0:T(8,128)(2,1)S(1)}, bf16[8,128,1024]{1,2,0:T(8,128)(2,1)}, u32[]{:S(2)}) copy-start(bf16[8,128,1024]{1,2,0:T(8,128)(2,1)} %fusion.13) | copy-start | bytes 6291460
  161.1 4.5 %copy-start.23 = (bf16[1024,512]{1,0:T(8,128)(2,1)S(1)}, bf16[1024,512]{1,0:T(8,128)(2,1)}, u32[]{:S(2)}) copy-start(bf16[1024,512]{1,0:T(8,128)(2,1)} %all-gather.9.cloned.1.call-done) | copy-start | bytes 3145732
  161.1 5.0 %copy-start.10 = (bf16[8,128,1024]{1,2,0:T(8,128)(2,1)S(1)}, bf16[8,128,1024]{1,2,0:T(8,128)(2,1)}, u32[]{:S(2)}) copy-start(bf16[8,128,1024]{1,2,0:T(8,128)(2,1)} %copy-done.9) | copy-start | bytes 6291460
  181.8 4.2 %copy-start.3 = (f32[1024,128,8]{1,0,2:T(8,128)}, f32[1024,128,8]{1,0,2:T(8,128)S(1)}, u32[]{:S(2)}) copy-start(f32[1024,128,8]{1,0,2:T(8,128)S(1)} %fusion.151) | copy-start | bytes 12582916
  290.8 74.0 %copy-start.37 = (f32[128]{0:T(128)S(1)}, f32[128]{0:T(128)}, u32[]{:S(2)}) copy-start(f32[128]{0:T(128)} %copy-done.36) | copy-start | bytes 1540
  290.9 74.1 %copy-start.38 = (f32[128]{0:T(128)S(1)}, f32[128]{0:T(128)}, u32[]{:S(2)}) copy-start(f32[128]{0:T(128)} %get-tuple-element.11) | copy-start | bytes 1540
  (25 other events, 70.5 us)
Sparse Core Ops, SparseCore 0:
  13.6 49.9 all-gather.8
  65.9 46.8 all-gather.10
  115.2 45.9 all-gather.4
  163.4 45.9 all-gather.6
  213.4 71.6 reduce-scatter.2
  288.6 71.7 reduce-scatter.4
where the time goes:
time: 379 us; the launch traced here: 374 us
  waiting for transfers between devices  215 us (57%)
  matrix products  90.5 us (24%)
  local copies, waits for them, and re-layouts  29.6 us (8%)
  other arithmetic  23.6 us (6%)
  between operations  14.9 us (4%)
    reduce_scatter x1, waiting for transfers between devices, body(): lax.psum_scatter(dvalue_terms.astype(jnp.bfloat16), 'ctx', scatter_dimens...  69.5 us
    reduce_scatter x1, waiting for transfers between devices, body(): lax.psum_scatter(dkey_terms.astype(jnp.bfloat16), 'ctx', scatter_dimensio...  59.2 us
    all_gather x1, waiting for transfers between devices, body(): lax.all_gather(bwd_values, 'ctx', axis=0, tiled=True)  44.6 us
    sub x4, matrix products, body(): expo = jnp.where(allowed[None], jnp.exp(scores - rowmax), 0.0)  21 us
    all_gather x1, waiting for transfers between devices, body(): value_piece = lax.all_gather(fwd_values, 'ctx', axis=0, tiled=True)  18.2 us
    dot_general x4, matrix products, body(): jnp.einsum('tgd,sd->gts', grad_grp, value_grp, preferred_element_type=jnp...  13 us
    unnamed x82, local copies, waits for them, and re-layouts  12.8 us
    ppermute x2, waiting for transfers between devices, shifted(): return lax.ppermute(block, axis, route)  12.7 us
  transfers between devices with their start and end apart: 8, of which 6 were waited for; matrix products, arithmetic and copies ran while one was open for 32% of the time, Pallas kernels for 0%

commit v1 on v0

--- a/solution.py
+++ b/solution.py
@@ -6,6 +6,15 @@
 HD = 128
 EPSILON = 1e-05
 NEGATIVE = -1e30
+
+
+def _set_column(array_here):
+    all_rows = []
+    for _ in range(jax.lax.axis_size("ctx")):
+        all_rows.append(array_here)
+    inter = jnp.stack(all_rows, 0)
+    x_next = jax.lax.all_to_all(inter, "ctx", 0, 0)
+    return jnp.concatenate(x_next, axis=0)
 
 
 def shifted(block, axis, distance):
@@ -88,7 +97,7 @@
         new_acc.append(product)
     bwd_key_all, bwd_value_all = (
         lax.all_gather(bwd_keys, "ctx", axis=0, tiled=True),
-        lax.all_gather(bwd_values, "ctx", axis=0, tiled=True),
+        _set_column(bwd_values),
     )
     attended = jnp.concatenate(new_acc, axis=0) / jnp.concatenate(new_total, axis=0)[:, :, None]
     attended = jnp.transpose(attended, (1, 0, 2)).reshape(tok_rows, width)

time: 379 us -> 336 us (0.89)
  waiting for transfers between devices: 215 us -> 153 us
  matrix products: 90.5 us -> 99.6 us
  starting transfers between devices: 0.4 us -> 8.31 us
    all_gather x1 -> x0, waiting for transfers between devices: 44.6 us -> none  [body(): lax.all_gather(bwd_values, 'ctx', axis=0, tiled=True)]
    all_gather x1, waiting for transfers between devices: 18.2 us -> 4.13 us  [body(): value_piece = lax.all_gather(fwd_values, 'ctx', axis=0, tiled=True)]
    sub x4, matrix products: 21 us -> 30.7 us  [body(): expo = jnp.where(allowed[None], jnp.exp(scores - rowmax), 0.0)]
    all_to_all x0 -> x1, starting transfers between devices: none -> 7.96 us  [_set_column(): x_next = jax.lax.all_to_all(inter, 'ctx', 0, 0)]
    unnamed x82 -> x80, local copies, waits for them, and re-layouts: 12.8 us -> 13 us
  transfers between devices with their start and end apart: 8 -> 8, of which waited for: 6 -> 5; matrix products, arithmetic and copies ran while one was open for 32% -> 41% of each run, Pallas kernels for 0% -> 0%
where the time goes in v1:
time: 336 us; the launch traced here: 330 us
  waiting for transfers between devices  153 us (46%)
  matrix products  99.6 us (30%)
  local copies, waits for them, and re-layouts  30.9 us (9%)
  other arithmetic  23.5 us (7%)
  between operations  14.5 us (4%)
  starting transfers between devices  8.31 us (2%)
    reduce_scatter x1, waiting for transfers between devices, body(): lax.psum_scatter(dvalue_terms.astype(jnp.bfloat16), 'ctx', scatter_dimens...  69.5 us
    reduce_scatter x1, waiting for transfers between devices, body(): lax.psum_scatter(dkey_terms.astype(jnp.bfloat16), 'ctx', scatter_dimensio...  59.2 us
    sub x4, matrix products, body(): expo = jnp.where(allowed[None], jnp.exp(scores - rowmax), 0.0)  30.7 us
    unnamed x80, local copies, waits for them, and re-layouts  13 us
    dot_general x4, matrix products, body(): jnp.einsum('tgd,sd->gts', grad_grp, value_grp, preferred_element_type=jnp...  12.9 us
    ppermute x2, waiting for transfers between devices, shifted(): return lax.ppermute(block, axis, route)  10.4 us
    all_gather x1, waiting for transfers between devices, body(): lax.all_gather(bwd_keys, 'ctx', axis=0, tiled=True)  10 us
    all_to_all x1, starting transfers between devices, _set_column(): x_next = jax.lax.all_to_all(inter, 'ctx', 0, 0)  7.96 us
  transfers between devices with their start and end apart: 8, of which 5 were waited for; matrix products, arithmetic and copies ran while one was open for 41% of the time, Pallas kernels for 0%

profile of v1, /device:TPU:0, one launch (start us, length us, event | category | flops | bytes accessed | tf_op | source)
XLA Modules:
  0.0 330.2 jit_solution(15862558604607109155)
XLA Ops:
  9.4 4.0 %fusion.121 = bf16[128,512]{1,0:T(8,128)(2,1)} fusion(bf16[1,4096,512]{2,1,0:T(8,128)(2,1)} %param.12, bf16[1,128,4096]{2,1,0:T(8,128)(2,1)} %param.10, f32[128]{0:T(128)S(1)} %get-tuple-element.12, f32[4096]{0:T(1024)} %bitcast.353), kind=kOutput, calls=%fused_computation.149 | convolution fusion | flops 539033600 | bytes 5390848 | tf_op jit(solution)/shard_map/dot_general | solution.py:51
  13.4 10.4 %collective-permute-done = bf16[1,128,4096]{2,1,0:T(8,128)(2,1)S(1)} collective-permute-done((bf16[1,128,4096]{2,1,0:T(8,128)(2,1)}, bf16[1,128,4096]{2,1,0:T(8,128)(2,1)S(1)}, u32[]{:S(2)}, u32[]{:S(2)}) %collective-permute-start) | collective-permute-done | bytes 1048608 | tf_op jit(solution)/shard_map/ppermute | solution.py:23
  24.1 3.6 %fusion.118 = bf16[128,512]{1,0:T(8,128)(2,1)} fusion(bf16[1,4096,512]{2,1,0:T(8,128)(2,1)} %param.12, bf16[1,128,4096]{2,1,0:T(8,128)(2,1)S(1)} %collective-permute-done, f32[4096]{0:T(1024)S(1)} %bitcast.354, f32[128]{0:T(128)S(1)} %add_rsqrt_fusion.1), kind=kOutput, calls=%fused_computation.148 | convolution fusion | flops 539033600 | bytes 5390848 | tf_op jit(solution)/shard_map/dot_general | solution.py:51
  32.0 8.0 %all-to-all-start = ((bf16[8,128,512]{2,1,0:T(8,128)(2,1)}), bf16[8,128,512]{2,1,0:T(8,128)(2,1)}, u32[]{:S(2)}, u32[]{:S(2)}) async-start(bf16[8,128,512]{2,1,0:T(8,128)(2,1)} %stack.2), calls=%async_computation | async-start | bytes 2097152 | tf_op jit(solution)/shard_map/all_to_all | solution.py:16
  45.0 3.8 %fusion.124 = bf16[128,512]{1,0:T(8,128)(2,1)} fusion(bf16[1,4096,512]{2,1,0:T(8,128)(2,1)} %param.13, bf16[1,128,4096]{2,1,0:T(8,128)(2,1)S(1)} %collective-permute-done, f32[4096]{0:T(1024)S(1)} %bitcast.356, f32[128]{0:T(128)S(1)} %add_rsqrt_fusion.1), kind=kOutput, calls=%fused_computation.150 | convolution fusion | flops 539033600 | bytes 5390848 | tf_op jit(solution)/shard_map/dot_general | solution.py:52
  55.1 4.2 %multiply_convert_fusion = (bf16[128,32,128]{2,0,1:T(8,128)(2,1)}, bf16[128,32,128]{2,0,1:T(8,128)(2,1)}) fusion(f32[128,32,128]{2,0,1:T(8,128)} %copy.40, f32[128]{0:T(128)S(1)} %get-tuple-element.12, f32[32,128]{1,0:T(8,128)S(1)} %bitcast.357, f32[128,32,128]{2,0,1:T(8,128)} %copy.29, f32[128]{0:T(128)S(1)} %add_rsqrt_fusion.1), kind=kLoop, calls=%fused_computation.95 | loop fusion | flops 3145728 | bytes 6308864 | tf_op jit(solution)/shard_map/convert_element_type | solution.py:50
  59.3 10.0 %all-gather.8.cloned.1.call-done = bf16[1024,512]{1,0:T(8,128)(2,1)} async-done(((bf16[128,512]{1,0:T(8,128)(2,1)}), bf16[1024,512]{1,0:T(8,128)(2,1)}) %all-gather.8.cloned.1.call-update) | async-done | bytes 1048592 | tf_op jit(solution)/shard_map/all_gather | solution.py:99
  69.3 4.7 %fusion.224 = (f32[8,128]{1,0:T(8,128)S(1)}, f32[8,128,1024]{1,2,0:T(8,128)}) fusion(pred[128,1024]{0,1:T(8,128)(4,1)S(1)} %get-tuple-element.13, bf16[128,32,128]{2,0,1:T(8,128)(2,1)} %get-tuple-element.9, bf16[1024,512]{1,0:T(8,128)(2,1)} %all-gather.8.cloned.1.call-done), kind=kOutput, calls=%fused_computation.247 | convolution fusion | flops 273679360 | bytes 4984832 | tf_op jit(solution)/shard_map/sub | solution.py:126
  74.0 3.2 fusion.8
  81.2 5.4 %fusion.219 = (f32[8,128]{1,0:T(8,128)}, f32[8,128,1024]{1,2,0:T(8,128)}) fusion(pred[128,1024]{0,1:T(8,128)(4,1)} %copy-done.26, bf16[128,32,128]{2,0,1:T(8,128)(2,1)} %get-tuple-element.9, bf16[1024,512]{1,0:T(8,128)(2,1)} %all-gather.8.cloned.1.call-done), kind=kOutput, calls=%fused_computation.246 | convolution fusion | flops 273679360 | bytes 4984832 | tf_op jit(solution)/shard_map/sub | solution.py:126
  86.7 3.2 fusion.5
  94.6 5.4 %fusion.229 = (f32[8,128]{1,0:T(8,128)}, f32[8,128,1024]{1,2,0:T(8,128)}) fusion(pred[128,1024]{0,1:T(8,128)(4,1)} %copy-done.26, bf16[128,32,128]{2,0,1:T(8,128)(2,1)} %get-tuple-element.9, bf16[1024,512]{1,0:T(8,128)(2,1)} %all-gather.8.cloned.1.call-done), kind=kOutput, calls=%fused_computation.248 | convolution fusion | flops 273679360 | bytes 4984832 | tf_op jit(solution)/shard_map/sub | solution.py:126
  100.0 3.3 fusion.11
  105.6 15.2 %fusion.234 = (f32[8,128]{1,0:T(8,128)}, f32[8,128,1024]{1,2,0:T(8,128)}) fusion(pred[128,1024]{0,1:T(8,128)(4,1)} %copy-done.26, bf16[128,32,128]{2,0,1:T(8,128)(2,1)} %get-tuple-element.9, bf16[1024,512]{1,0:T(8,128)(2,1)} %all-gather.8.cloned.1.call-done), kind=kOutput, calls=%fused_computation.249 | convolution fusion | flops 273679360 | bytes 4984832 | tf_op jit(solution)/shard_map/sub | solution.py:126
  120.8 3.2 fusion.14
  139.2 3.0 copy.54
  142.2 3.1 fusion.102
  158.9 3.2 fusion.37
  162.1 4.1 %all-gather.6.cloned.1.call-done = bf16[1024,512]{1,0:T(8,128)(2,1)} async-done(((bf16[128,512]{1,0:T(8,128)(2,1)}), bf16[1024,512]{1,0:T(8,128)(2,1)}) %all-gather.6.cloned.1.call-update) | async-done | bytes 1048592 | tf_op jit(solution)/shard_map/all_gather | solution.py:61
  166.2 3.5 %fusion.72 = f32[8,128,128]{1,2,0:T(8,128)S(1)} fusion(f32[1024,128,8]{1,0,2:T(8,128)} %copy-done.19, f32[8,128]{1,0:T(8,128)S(1)} %broadcast_maximum_fusion.3, pred[128,1024]{0,1:T(8,128)(4,1)S(1)} %get-tuple-element.14, bf16[1024,512]{1,0:T(8,128)(2,1)} %all-gather.6.cloned.1.call-done), kind=kOutput, calls=%fused_computation.111 | convolution fusion | flops 273678336 | bytes 5115904 | tf_op jit(solution)/shard_map/gts,sd->gtd/dot_general | solution.py:91
  182.8 59.2 %reduce-scatter.3.cloned.1.call-done = bf16[128,512]{1,0:T(8,128)(2,1)} async-done(((bf16[1024,512]{1,0:T(8,128)(2,1)}), bf16[128,512]{1,0:T(8,128)(2,1)}) %reduce-scatter.3.cloned.1.call-update) | async-done | bytes 131088 | tf_op jit(solution)/shard_map/reduce_scatter | solution.py:148
  242.0 5.7 %convolution_add_fusion.1 = f32[128,4096]{1,0:T(8,128)} fusion(f32[128,4096]{1,0:T(8,128)} %copy.54, bf16[128,512]{1,0:T(8,128)(2,1)} %reduce-scatter.3.cloned.1.call-done, bf16[1,4096,512]{2,1,0:T(8,128)(2,1)} %param.12), kind=kOutput, calls=%fused_computation.6 | convolution fusion | flops 537395200 | bytes 8519680 | tf_op jit(solution)/shard_map/dot_general | solution.py:155
  247.8 69.5 %reduce-scatter.5.cloned.1.call-done = bf16[128,512]{1,0:T(8,128)(2,1)} async-done(((bf16[1024,512]{1,0:T(8,128)(2,1)}), bf16[128,512]{1,0:T(8,128)(2,1)}) %reduce-scatter.5.cloned.1.call-update) | async-done | bytes 131088 | tf_op jit(solution)/shard_map/reduce_scatter | solution.py:151
  317.3 4.5 %fusion.47 = (f32[128]{0:T(128)S(1)}, f32[128,4096]{1,0:T(8,128)S(1)}) fusion(bf16[1,128,4096]{2,1,0:T(8,128)(2,1)S(1)} %copy-done, f32[128,4096]{1,0:T(8,128)} %convolution_add_fusion.1, bf16[128,512]{1,0:T(8,128)(2,1)} %reduce-scatter.5.cloned.1.call-done, bf16[1,4096,512]{2,1,0:T(8,128)(2,1)} %param.13, f32[4096]{0:T(1024)S(1)} %bitcast.358), kind=kOutput, calls=%fused_computation.79 | convolution fusion | flops 539492224 | bytes 9585152 | tf_op jit(solution)/shard_map/dot_general | solution.py:158
  (144 shorter events, 72.3 us)
Async XLA Ops:
  7.2 17.0 %copy-start.27 = (f32[1,4096]{1,0:T(1,128)S(1)}, f32[1,4096]{1,0:T(1,128)}, u32[]{:S(2)}) copy-start(f32[1,4096]{1,0:T(1,128)} %param.11) | copy-start | bytes 49156
  7.2 62.2 %all-gather.8.cloned.1.call-start = ((), (), s32[]{:S(2)}) async-start(), calls=%async_computation.5 | async-start | bytes 1179648 | tf_op jit(solution)/shard_map/all_gather | solution.py:99
  7.2 16.6 %collective-permute-start = (bf16[1,128,4096]{2,1,0:T(8,128)(2,1)}, bf16[1,128,4096]{2,1,0:T(8,128)(2,1)S(1)}, u32[]{:S(2)}, u32[]{:S(2)}) collective-permute-start(bf16[1,128,4096]{2,1,0:T(8,128)(2,1)} %param.8), channel_id=1, source_target_pairs={{120,0},{0,8},{8,16},{16,24},{24,32},{32,40},{40,48},{48,56},{56,6... | collective-permute-start | bytes 3145736 | tf_op jit(solution)/shard_map/ppermute | solution.py:23
  9.4 45.7 %copy-start.36 = (f32[128]{0:T(128)}, f32[128]{0:T(128)S(1)}, u32[]{:S(2)}) copy-start(f32[128]{0:T(128)S(1)} %get-tuple-element.12) | copy-start | bytes 1540
  13.3 14.6 %copy-start = (bf16[1,128,4096]{2,1,0:T(8,128)(2,1)S(1)}, bf16[1,128,4096]{2,1,0:T(8,128)(2,1)}, u32[]{:S(2)}) copy-start(bf16[1,128,4096]{2,1,0:T(8,128)(2,1)} %param.10) | copy-start | bytes 3145732
  13.3 136.8 %all-gather.4.cloned.1.call-start = ((), (), s32[]{:S(2)}) async-start(), calls=%async_computation.3 | async-start | bytes 1179648 | tf_op jit(solution)/shard_map/all_gather | solution.py:60
  27.8 25.6 %collective-permute-start.1 = (bf16[1,128,4096]{2,1,0:T(8,128)(2,1)}, bf16[1,128,4096]{2,1,0:T(8,128)(2,1)S(1)}, u32[]{:S(2)}, u32[]{:S(2)}) collective-permute-start(bf16[1,128,4096]{2,1,0:T(8,128)(2,1)} %param.9), channel_id=1, source_target_pairs={{8,0},{16,8},{24,16},{32,24},{40,32},{48,40},{56,48},{64,56},{72,6... | collective-permute-start | bytes 3145736 | tf_op jit(solution)/shard_map/ppermute | solution.py:23
  30.8 10.7 %copy-start.29 = (s32[1024]{0:T(1024)S(1)}, s32[1024]{0:T(1024)}, u32[]{:S(2)}) copy-start(s32[1024]{0:T(1024)} %param.14) | copy-start | bytes 12292
  30.9 10.8 %copy-start.28 = (s32[1024]{0:T(1024)S(1)}, s32[1024]{0:T(1024)}, u32[]{:S(2)}) copy-start(s32[1024]{0:T(1024)} %param.15) | copy-start | bytes 12292
  32.0 42.1 %all-to-all-start = ((bf16[8,128,512]{2,1,0:T(8,128)(2,1)}), bf16[8,128,512]{2,1,0:T(8,128)(2,1)}, u32[]{:S(2)}, u32[]{:S(2)}) async-start(bf16[8,128,512]{2,1,0:T(8,128)(2,1)} %stack.2), calls=%async_computation | async-start | bytes 2097152 | tf_op jit(solution)/shard_map/all_to_all | solution.py:16
  39.9 126.3 %all-gather.6.cloned.1.call-start = ((), (), s32[]{:S(2)}) async-start(), calls=%async_computation.4 | async-start | bytes 1179648 | tf_op jit(solution)/shard_map/all_gather | solution.py:61
  45.0 24.3 %copy-start.26 = (pred[128,1024]{0,1:T(8,128)(4,1)}, pred[128,1024]{0,1:T(8,128)(4,1)S(1)}, u32[]{:S(2)}) copy-start(pred[128,1024]{0,1:T(8,128)(4,1)S(1)} %get-tuple-element.13) | copy-start | bytes 393220
  53.3 188.7 %reduce-scatter.3.cloned.1.call-start = ((), (), s32[]{:S(2)}) async-start(), calls=%async_computation.6 | async-start | bytes 1179648 | tf_op jit(solution)/shard_map/reduce_scatter | solution.py:148
  120.8 4.6 %copy-start.15 = (f32[8,128,1024]{1,2,0:T(8,128)S(1)}, f32[8,128,1024]{1,2,0:T(8,128)}, u32[]{:S(2)}) copy-start(f32[8,128,1024]{1,2,0:T(8,128)} %get-tuple-element.31) | copy-start | bytes 12582916
  120.8 4.6 %copy-start.34 = (f32[8,128]{1,0:T(8,128)S(1)}, f32[8,128]{1,0:T(8,128)}, u32[]{:S(2)}) copy-start(f32[8,128]{1,0:T(8,128)} %get-tuple-element.30) | copy-start | bytes 12292
  132.1 185.2 %reduce-scatter.5.cloned.1.call-start = ((), (), s32[]{:S(2)}) async-start(), calls=%async_computation.7 | async-start | bytes 1179648 | tf_op jit(solution)/shard_map/reduce_scatter | solution.py:151
  132.1 4.5 %copy-start.8 = (bf16[8,128,1024]{1,2,0:T(8,128)(2,1)S(1)}, bf16[8,128,1024]{1,2,0:T(8,128)(2,1)}, u32[]{:S(2)}) copy-start(bf16[8,128,1024]{1,2,0:T(8,128)(2,1)} %fusion.13) | copy-start | bytes 6291460
  132.1 4.5 %copy-start.23 = (bf16[1024,512]{1,0:T(8,128)(2,1)S(1)}, bf16[1024,512]{1,0:T(8,128)(2,1)}, u32[]{:S(2)}) copy-start(bf16[1024,512]{1,0:T(8,128)(2,1)} %all-gather.8.cloned.1.call-done) | copy-start | bytes 3145732
  132.2 5.0 %copy-start.10 = (bf16[8,128,1024]{1,2,0:T(8,128)(2,1)S(1)}, bf16[8,128,1024]{1,2,0:T(8,128)(2,1)}, u32[]{:S(2)}) copy-start(bf16[8,128,1024]{1,2,0:T(8,128)(2,1)} %copy-done.9) | copy-start | bytes 6291460
  142.2 3.8 %copy-start.35 = (f32[8,128]{1,0:T(8,128)S(1)}, f32[8,128]{1,0:T(8,128)}, u32[]{:S(2)}) copy-start(f32[8,128]{1,0:T(8,128)} %get-tuple-element.30) | copy-start | bytes 12292
  152.8 4.2 %copy-start.3 = (f32[1024,128,8]{1,0,2:T(8,128)}, f32[1024,128,8]{1,0,2:T(8,128)S(1)}, u32[]{:S(2)}) copy-start(f32[1024,128,8]{1,0,2:T(8,128)S(1)} %fusion.151) | copy-start | bytes 12582916
  166.2 3.8 %copy-start.39 = (bf16[1024,512]{1,0:T(8,128)(2,1)S(1)}, bf16[1024,512]{1,0:T(8,128)(2,1)}, u32[]{:S(2)}) copy-start(bf16[1024,512]{1,0:T(8,128)(2,1)} %all-gather.6.cloned.1.call-done) | copy-start | bytes 3145732
  247.8 74.0 %copy-start.37 = (f32[128]{0:T(128)S(1)}, f32[128]{0:T(128)}, u32[]{:S(2)}) copy-start(f32[128]{0:T(128)} %copy-done.36) | copy-start | bytes 1540
  247.8 74.0 %copy-start.38 = (f32[128]{0:T(128)S(1)}, f32[128]{0:T(128)}, u32[]{:S(2)}) copy-start(f32[128]{0:T(128)} %get-tuple-element.11) | copy-start | bytes 1540
  (24 other events, 65.7 us)
Sparse Core Ops, SparseCore 0:
  13.5 55.8 all-gather.7
  71.7 46.2 all-gather.3
  120.3 45.9 all-gather.5
  170.3 71.6 reduce-scatter.2
  245.5 71.7 reduce-scatter.4
